TPU v7x, 512 devices: a whole 4x8x8 slice. The times are simulated.
512 devices in a mesh: ctx: 64 (over x, y, core), fsdp: 8 (over z).
Axes of the slice: x: 4, y: 8, z: 8, core: 2. Of those that a mesh axis runs over, the one named last changes fastest.
Arguments:
- outer_gate: bfloat16 [2048, 16384], P('fsdp', 'ctx'), may hold values from -6 to 6
- inner_gate: bfloat16 [2048, 16384], P('fsdp', 'ctx'), may hold values from -6 to 6
- value_stream: bfloat16 [2048, 16384], P('fsdp', 'ctx'), may hold values from -6 to 6
- grad_output: bfloat16 [2048, 16384], P('fsdp', 'ctx'), may hold values from -6 to 6
- filters: float32 [128, 128], P('fsdp', 'ctx'), may hold values from -0.5 to 0.5
- feature_taps: float32 [3, 3, 2048], P(None, None, ('ctx', 'fsdp')), may hold values from -3 to 3
- skip_gain: float32 [2048], P(('ctx', 'fsdp')), may hold values from -4 to 4
Outputs:
- gated_out: bfloat16 [2048, 16384], P('fsdp', 'ctx')
- grad_outer: bfloat16 [2048, 16384], P('fsdp', 'ctx')
- grad_inner: bfloat16 [2048, 16384], P('fsdp', 'ctx')
- grad_value: bfloat16 [2048, 16384], P('fsdp', 'ctx')
- grad_filters: float32 [128, 128], P('fsdp', 'ctx')
- grad_taps: float32 [3, 3, 2048], P(None, None, ('ctx', 'fsdp'))
- grad_skip: float32 [2048], P(('ctx', 'fsdp'))
All inputs are finite; a program needn't handle non-finite values.
Results may differ from a plain program's by a relative error of at most 0.03.
Values may be sent and summed in bfloat16 or wider, within the bound.
No kernel may reach another device: no remote copies, remote signals or barrier semaphores. Data moves between devices by JAX's collectives and lax.ppermute only.
A program may use at most 64 MiB of HBM per device.

v0:
```python
import math
import jax
import jax.numpy as jnp
from jax import lax
from jax.sharding import PartitionSpec as P


def passed_along(shard, axis, by):
    devices = lax.axis_size(axis)
    pairs = [(i, i + by) for i in range(devices) if 0 <= i + by < devices]
    return lax.ppermute(shard, axis, pairs)


def featurize(extended, tap_gains):
    block_len = extended.shape[1] - 2
    result = tap_gains[0][:, None] * extended[:, 2:]
    result = result + tap_gains[1][:, None] * extended[:, 1 : block_len + 1]
    return result + tap_gains[2][:, None] * extended[:, :block_len]


def carry_back(extended, tap_gains):
    block_len = extended.shape[1] - 2
    result = tap_gains[0][:, None] * extended[:, :block_len]
    result = result + tap_gains[1][:, None] * extended[:, 1 : block_len + 1]
    return result + tap_gains[2][:, None] * extended[:, 2:]


def tap_sums(grad_rows, extended):
    block_len = grad_rows.shape[1]
    weighted = grad_rows.astype(jnp.float32)
    return jnp.stack(
        [
            jnp.sum(
                weighted * extended[:, 2 - shift_by : 2 - shift_by + block_len].astype(jnp.float32),
                axis=1,
            )
            for shift_by in range(3)
        ]
    )


def toeplitz_rows(filters_low, block_len):
    groups, taps_count = filters_low.shape
    window = block_len + taps_count - 1
    filter_row = jnp.concatenate(
        [filters_low[:, ::-1], jnp.zeros((groups, window + 1 - taps_count), filters_low.dtype)],
        axis=1,
    )
    flattened = jnp.tile(filter_row, (1, block_len))[:, : block_len * window]
    return flattened.reshape(groups, block_len, window)


def skew_sum(cross_terms, taps_count):
    groups, block_len, window = cross_terms.shape
    flattened = jnp.pad(cross_terms.reshape(groups, block_len * window), ((0, 0), (0, block_len)))
    return jnp.sum(flattened.reshape(groups, block_len, window + 1)[:, :, :taps_count], axis=1)[
        :, ::-1
    ]


def block_windows(extended, sub_len, reach_cols, groups):
    channels = extended.shape[0]
    block_len = extended.shape[1] - reach_cols
    count = block_len // sub_len
    lead = extended[:, :block_len].reshape(channels, count, sub_len)[:, :, :reach_cols]
    main = extended[:, reach_cols:].reshape(channels, count, sub_len)
    joined = jnp.concatenate([lead, main], axis=2)
    return joined.reshape(groups, channels // groups, count, sub_len + reach_cols)


def shards(outer_gate, inner_gate, value_stream, grad_output, filters, feature_taps, skip_gain):
    filters_all = lax.all_gather(filters, "ctx", axis=1, tiled=True)
    taps_every, skip_every = (
        lax.all_gather(feature_taps, ("ctx", "fsdp"), axis=2, tiled=True),
        lax.all_gather(skip_gain, ("ctx", "fsdp"), axis=0, tiled=True),
    )
    channels, block_len = outer_gate.shape
    chan_start = lax.axis_index("fsdp") * channels
    taps_all = lax.dynamic_slice_in_dim(taps_every, chan_start, channels, 2)
    skip_all = lax.dynamic_slice_in_dim(skip_every, chan_start, channels, 0)
    groups, taps_count = filters_all.shape
    group_size = channels // groups
    reach_cols = taps_count - 1
    count = block_len // block_len
    window = block_len + reach_cols
    feature_rims = passed_along(
        (
            outer_gate[:, block_len - 2 :],
            inner_gate[:, block_len - 2 :],
            value_stream[:, block_len - 2 :],
        ),
        "ctx",
        1,
    )
    outer_ext = jnp.concatenate([feature_rims[0], outer_gate], axis=1)
    inner_ext = jnp.concatenate([feature_rims[1], inner_gate], axis=1)
    value_ext = jnp.concatenate([feature_rims[2], value_stream], axis=1)
    outer_feat = featurize(outer_ext.astype(jnp.float32), taps_all[0])
    inner_feat = featurize(inner_ext.astype(jnp.float32), taps_all[1])
    value_feat = featurize(value_ext.astype(jnp.float32), taps_all[2])
    product = (inner_feat * value_feat).astype(jnp.bfloat16)
    product_rim = passed_along(product[:, block_len - reach_cols :], "ctx", 1)
    product_ext = jnp.concatenate([product_rim, product], axis=1)
    toeplitz = toeplitz_rows(filters_all.astype(jnp.bfloat16), block_len)
    windows = block_windows(product_ext, block_len, reach_cols, groups)
    convolved = jnp.einsum(
        "gcns,gts->gcnt", windows, toeplitz, preferred_element_type=jnp.float32
    ).reshape(channels, block_len)
    mixed = convolved + skip_all[:, None] * product.astype(jnp.float32)
    gated_out = (outer_feat * mixed).astype(jnp.bfloat16)
    upstream = grad_output.astype(jnp.float32)
    grad_mixed = (upstream * outer_feat).astype(jnp.bfloat16)
    grad_outer_feat = (upstream * mixed).astype(jnp.bfloat16)
    grad_groups = grad_mixed.reshape(groups, group_size, count, block_len)
    direct_term = skip_all[:, None] * grad_mixed.astype(jnp.float32)
    ahead_rims = passed_along((grad_mixed[:, :reach_cols], grad_outer_feat[:, :2]), "ctx", -1)
    mixed_ext = jnp.concatenate([grad_mixed, ahead_rims[0]], axis=1)
    flipped = block_windows(mixed_ext[:, ::-1], block_len, reach_cols, groups)
    reversed_out = jnp.einsum(
        "gcns,gts->gcnt", flipped, toeplitz, preferred_element_type=jnp.float32
    ).reshape(channels, block_len)
    grad_product = reversed_out[:, ::-1] + direct_term
    grad_inner_feat = (grad_product * value_feat).astype(jnp.bfloat16)
    grad_value_feat = (grad_product * inner_feat).astype(jnp.bfloat16)
    later_rims = passed_along((grad_inner_feat[:, :2], grad_value_feat[:, :2]), "ctx", -1)
    grad_outer = carry_back(
        jnp.concatenate([grad_outer_feat, ahead_rims[1]], axis=1).astype(jnp.float32), taps_all[0]
    )
    grad_inner = carry_back(
        jnp.concatenate([grad_inner_feat, later_rims[0]], axis=1).astype(jnp.float32), taps_all[1]
    )
    grad_value = carry_back(
        jnp.concatenate([grad_value_feat, later_rims[1]], axis=1).astype(jnp.float32), taps_all[2]
    )
    grad_scale = 1.0 / math.sqrt(lax.axis_size("ctx") * block_len)
    group_block = math.gcd(groups, 4)

    def cross_block(block_pair):
        grad_part, window_part = block_pair
        cross_terms = jnp.einsum(
            "gcnt,gcns->gts", grad_part, window_part, preferred_element_type=jnp.float32
        )
        return skew_sum(cross_terms, taps_count)

    filter_part = lax.map(
        cross_block,
        (
            grad_groups.reshape(groups // group_block, group_block, group_size, count, block_len),
            windows.reshape(groups // group_block, group_block, group_size, count, window),
        ),
    )
    filter_part = grad_scale * filter_part.reshape(groups, taps_count)
    skip_part = grad_scale * jnp.sum(
        grad_mixed.astype(jnp.float32) * product.astype(jnp.float32), axis=1
    )
    taps_part = grad_scale * jnp.stack(
        [
            tap_sums(grad_outer_feat, outer_ext),
            tap_sums(grad_inner_feat, inner_ext),
            tap_sums(grad_value_feat, value_ext),
        ]
    )
    filter_share = lax.psum_scatter(filter_part, "ctx", scatter_dimension=1, tiled=True)
    whole_taps = lax.dynamic_update_slice_in_dim(
        jnp.zeros(taps_every.shape, jnp.float32), taps_part, chan_start, 2
    )
    whole_skip = lax.dynamic_update_slice_in_dim(
        jnp.zeros(skip_every.shape, jnp.float32), skip_part, chan_start, 0
    )
    taps_share, skip_share = (
        lax.psum_scatter(whole_taps, ("ctx", "fsdp"), scatter_dimension=2, tiled=True),
        lax.psum_scatter(whole_skip, ("ctx", "fsdp"), scatter_dimension=0, tiled=True),
    )
    return (
        gated_out,
        grad_outer.astype(jnp.bfloat16),
        grad_inner.astype(jnp.bfloat16),
        grad_value.astype(jnp.bfloat16),
        filter_share,
        taps_share,
        skip_share,
    )


def solution(mesh):
    return jax.shard_map(
        shards,
        mesh=mesh,
        in_specs=(
            P("fsdp", "ctx"),
            P("fsdp", "ctx"),
            P("fsdp", "ctx"),
            P("fsdp", "ctx"),
            P("fsdp", "ctx"),
            P(None, None, ("ctx", "fsdp")),
            P(("ctx", "fsdp")),
        ),
        out_specs=(
            P("fsdp", "ctx"),
            P("fsdp", "ctx"),
            P("fsdp", "ctx"),
            P("fsdp", "ctx"),
            P("fsdp", "ctx"),
            P(None, None, ("ctx", "fsdp")),
            P(("ctx", "fsdp")),
        ),
        check_vma=False,
    )
```

profile of v0, /device:TPU:1, one launch (start us, length us, event | category | flops | bytes accessed | tf_op | source)
XLA Modules:
  0.0 771.6 jit_solution(13353346881446021520)
XLA Ops:
  7.2 1.6 slice.185
  8.8 4.6 collective-permute-start
  13.4 1.6 slice.199
  14.9 1.9 collective-permute-start.2
  16.9 1.6 slice.192
  18.4 3.6 collective-permute-start.1
  22.8 142.3 %all_gather.9 = f32[3,3,2048]{1,0,2:T(4,128)} all-gather(f32[3,3,4]{1,0,2:T(4,128)S(1)} %copy.30), channel_id=1, replica_groups=mesh['ctx'=64,'fsdp'=8] {'ctx','fsdp'}, dimensions={2}, use_global_device_ids=true | all-gather | bytes 73872 | tf_op jit(solution)/shard_map/all_gather | solution.py:74
  165.2 35.0 %all-gather = bf16[64,2,16]{2,1,0:T(2,128)(2,1)S(1)} all-gather(bf16[1,2,16]{2,1,0:T(2,128)(2,1)S(1)} %bitcast_convert_fusion), channel_id=1, replica_groups=mesh['ctx'=64,'fsdp'=8] {'ctx'}, dimensions={0}, use_global_device_ids=true | all-gather | bytes 4160 | tf_op jit(solution)/shard_map/all_gather | solution.py:72
  200.5 1.9 copy.41
  202.4 11.8 %dynamic-slice_reduce_fusion.2 = (f32[256]{0:T(256)S(1)}, f32[256]{0:T(256)S(1)}, f32[256]{0:T(256)}, f32[256]{0:T(256)}, f32[256]{0:T(256)}, /*index=5*/f32[256]{0:T(256)}, f32[256]{0:T(256)}, f32[256]{0:T(256)}, f32[256]{0:T(256)}) fusion(f32[3,3,2048]{1,0,2:T(4,128)} %all_gather.9, s32[]{:T(128)S(6)} %add.97, s32[]{:T(128)S(6)} %select_n.2, s32[]{:T(128)S(6)} %add.96), kind=kLoop, calls=%fused_computation.115 | loop fusion | bytes 18444 | tf_op jit(solution)/shard_map/slice | solution.py:16
  214.2 1.9 slice.244
  216.1 9.4 %reshape.115 = bf16[16,256,383]{2,1,0:T(8,128)(2,1)S(1)} reshape(bf16[16,98048]{1,0:T(8,128)(2,1)} %slice.244) | data formatting | bytes 6275072 | tf_op jit(solution)/shard_map/reshape | solution.py:50
  231.2 2.6 fusion.10
  234.6 2.9 collective-permute-start.3
  239.8 95.0 %all-reduce.6 = (f32[2048]{0:T(1024)}, f32[2048]{0:T(1024)}) all-reduce(f32[2048]{0:T(1024)S(1)} %dynamic-update-slice, f32[2048]{0:T(1024)S(1)} %multiply_dynamic-update-slice_fusion), channel_id=1, replica_groups=mesh['ctx'=64,'fsdp'=8] {'ctx','fsdp'}, use_global_device_ids=true, to_apply=%add.2 | all-reduce | flops 4096 | bytes 32768
  335.6 2.6 collective-permute-start.5
  341.3 2.5 fusion.12
  345.1 1.9 collective-permute-start.4
  349.5 2.5 fusion.41
  352.1 1.9 rev.14
  354.0 2.6 fusion.18
  357.3 1.9 collective-permute-start.6
  359.8 1.9 collective-permute-start.7
  361.8 1.6 pad_maximum_fusion.3
  363.4 15.8 %while.12 = (s32[]{:T(128)}, f32[4,4,128]{2,1,0:T(4,128)}, bf16[4,4,16,1,256]{4,2,1,3,0:T(8,128)(2,1)S(1)}, bf16[4,4,16,1,383]{4,2,1,3,0:T(8,128)(2,1)}, s32[]{:T(128)}, /*index=5*/f32[]{:T(128)}) while((s32[]{:T(128)}, f32[4,4,128]{2,1,0:T(4,128)}, bf16[4,4,16,1,256]{4,2,1,3,0:T(8,128)(2,1)S(1)}, bf16[4,4,16,1,383]{4,2,1,3,0:T(8,128)(2,1)}, ...), condition=%wide.region_2.3_spmd, body=%wide.region_0.2_spmd.sunk | while | flops 12680706 | bytes 11611221 | solution.py:145
  364.7 1.6 reshape.140
  368.6 1.6 reshape.140
  372.6 1.6 reshape.140
  376.5 1.6 reshape.140
  380.0 126.0 %all-reduce.3 = f32[16,128]{1,0:T(8,128)S(1)} all-reduce(f32[16,128]{1,0:T(8,128)S(1)} %bitcast.98), channel_id=2, replica_groups=mesh['ctx'=64,'fsdp'=8] {'ctx'}, use_global_device_ids=true, to_apply=%region_3.4.clone | all-reduce | flops 2048 | bytes 16384
  509.1 1.6 fusion.27
  514.6 248.8 %all-reduce.9.cloned.1.call-done = f32[3,3,2048]{2,1,0:T(4,128)} async-done(((f32[3,3,2048]{2,1,0:T(4,128)}), f32[3,3,2048]{2,1,0:T(4,128)}) %all-reduce.9.cloned.1.call-update) | async-done | bytes 73744
  (116 shorter events, 36.5 us)
Async XLA Ops:
  7.2 158.0 %copy-start.19 = (f32[16,2]{0,1:T(2,128)S(1)}, f32[16,2]{0,1:T(2,128)}, u32[]{:S(2)}) copy-start(f32[16,2]{0,1:T(2,128)} %param.13) | copy-start | bytes 388
  7.2 756.2 %all-reduce.9.cloned.1.call-start = ((), (), s32[]{:S(2)}) async-start(), calls=%async_computation | async-start | bytes 196608
  8.8 221.4 %collective-permute-start = (bf16[256,2]{1,0:T(8,128)(2,1)}, bf16[256,2]{1,0:T(8,128)(2,1)}, u32[]{:S(2)}, u32[]{:S(2)}) collective-permute-start(bf16[256,2]{1,0:T(8,128)(2,1)} %slice.185), channel_id=1, source_target_pairs={{0,8},{8,16},{16,24},{24,32},{32,40},{40,48},{48,56},{56,64},{64,7... | collective-permute-start | bytes 3080 | tf_op jit(solution)/shard_map/ppermute | solution.py:11
  14.9 213.3 %collective-permute-start.2 = (bf16[256,2]{1,0:T(8,128)(2,1)}, bf16[256,2]{1,0:T(8,128)(2,1)}, u32[]{:S(2)}, u32[]{:S(2)}) collective-permute-start(bf16[256,2]{1,0:T(8,128)(2,1)} %slice.199), channel_id=1, source_target_pairs={{0,8},{8,16},{16,24},{24,32},{32,40},{40,48},{48,56},{56,64},{64,7... | collective-permute-start | bytes 3080 | tf_op jit(solution)/shard_map/ppermute | solution.py:11
  18.4 210.8 %collective-permute-start.1 = (bf16[256,2]{1,0:T(8,128)(2,1)}, bf16[256,2]{1,0:T(8,128)(2,1)}, u32[]{:S(2)}, u32[]{:S(2)}) collective-permute-start(bf16[256,2]{1,0:T(8,128)(2,1)} %slice.192), channel_id=1, source_target_pairs={{0,8},{8,16},{16,24},{24,32},{32,40},{40,48},{48,56},{56,64},{64,7... | collective-permute-start | bytes 3080 | tf_op jit(solution)/shard_map/ppermute | solution.py:11
  214.2 17.0 %copy-start.10 = (f32[256]{0:T(256)}, f32[256]{0:T(256)S(1)}, u32[]{:S(2)}) copy-start(f32[256]{0:T(256)S(1)} %get-tuple-element.98) | copy-start | bytes 3076
  214.2 17.0 %copy-start.12 = (f32[256]{0:T(256)}, f32[256]{0:T(256)S(1)}, u32[]{:S(2)}) copy-start(f32[256]{0:T(256)S(1)} %get-tuple-element.99) | copy-start | bytes 3076
  216.1 12.2 %copy-start.4 = (bf16[256,256]{1,0:T(8,128)(2,1)S(1)}, bf16[256,256]{1,0:T(8,128)(2,1)}, u32[]{:S(2)}) copy-start(bf16[256,256]{1,0:T(8,128)(2,1)} %param.11) | copy-start | bytes 393220
  216.1 13.2 %copy-start.5 = (bf16[256,256]{1,0:T(8,128)(2,1)S(1)}, bf16[256,256]{1,0:T(8,128)(2,1)}, u32[]{:S(2)}) copy-start(bf16[256,256]{1,0:T(8,128)(2,1)} %param.10) | copy-start | bytes 393220
  216.1 14.2 %copy-start.1 = (bf16[256,256]{1,0:T(8,128)(2,1)S(1)}, bf16[256,256]{1,0:T(8,128)(2,1)}, u32[]{:S(2)}) copy-start(bf16[256,256]{1,0:T(8,128)(2,1)} %param.9) | copy-start | bytes 393220
  234.6 104.9 %collective-permute-start.3 = (bf16[256,127]{1,0:T(8,128)(2,1)}, bf16[256,127]{1,0:T(8,128)(2,1)}, u32[]{:S(2)}, u32[]{:S(2)}) collective-permute-start(bf16[256,127]{1,0:T(8,128)(2,1)} %slice.242), channel_id=1, source_target_pairs={{0,8},{8,16},{16,24},{24,32},{32,40},{40,48},{48,56},{56,64},{64,7... | collective-permute-start | bytes 195080 | tf_op jit(solution)/shard_map/ppermute | solution.py:11
  334.8 6.5 copy-start
  334.8 6.5 copy-start.8
  335.6 11.4 %collective-permute-start.5 = (bf16[256,127]{1,0:T(8,128)(2,1)}, bf16[256,127]{1,0:T(8,128)(2,1)S(1)}, u32[]{:S(2)}, u32[]{:S(2)}) collective-permute-start(bf16[256,127]{1,0:T(8,128)(2,1)} %slice.249), channel_id=1, source_target_pairs={{8,0},{16,8},{24,16},{32,24},{40,32},{48,40},{56,48},{64,56},{72,6... | collective-permute-start | bytes 195080 | tf_op jit(solution)/shard_map/ppermute | solution.py:11
  340.4 4.7 copy-start.7
  343.8 0.7 copy-start.2
  345.1 163.1 %collective-permute-start.4 = (bf16[256,2]{1,0:T(8,128)(2,1)}, bf16[256,2]{1,0:T(8,128)(2,1)}, u32[]{:S(2)}, u32[]{:S(2)}) collective-permute-start(bf16[256,2]{1,0:T(8,128)(2,1)} %slice.245), channel_id=1, source_target_pairs={{8,0},{16,8},{24,16},{32,24},{40,32},{48,40},{56,48},{64,56},{72,6... | collective-permute-start | bytes 3080 | tf_op jit(solution)/shard_map/ppermute | solution.py:11
  356.6 6.8 copy-start.6
  357.3 153.4 %collective-permute-start.6 = (bf16[256,2]{1,0:T(8,128)(2,1)}, bf16[256,2]{1,0:T(8,128)(2,1)}, u32[]{:S(2)}, u32[]{:S(2)}) collective-permute-start(bf16[256,2]{1,0:T(8,128)(2,1)} %slice.251), channel_id=1, source_target_pairs={{8,0},{16,8},{24,16},{32,24},{40,32},{48,40},{56,48},{64,56},{72,6... | collective-permute-start | bytes 3080 | tf_op jit(solution)/shard_map/ppermute | solution.py:11
  359.8 152.9 %collective-permute-start.7 = (bf16[256,2]{1,0:T(8,128)(2,1)}, bf16[256,2]{1,0:T(8,128)(2,1)}, u32[]{:S(2)}, u32[]{:S(2)}) collective-permute-start(bf16[256,2]{1,0:T(8,128)(2,1)} %slice.255), channel_id=1, source_target_pairs={{8,0},{16,8},{24,16},{32,24},{40,32},{48,40},{56,48},{64,56},{72,6... | collective-permute-start | bytes 3080 | tf_op jit(solution)/shard_map/ppermute | solution.py:11
  363.4 144.8 %copy-start.3 = (bf16[256,256]{1,0:T(8,128)(2,1)S(1)}, bf16[256,256]{1,0:T(8,128)(2,1)}, u32[]{:S(2)}) copy-start(bf16[256,256]{1,0:T(8,128)(2,1)} %copy-done.2) | copy-start | bytes 393220
  363.4 145.7 %copy-start.18 = (f32[256]{0:T(256)S(1)}, f32[256]{0:T(256)}, u32[]{:S(2)}) copy-start(f32[256]{0:T(256)} %get-tuple-element.103) | copy-start | bytes 3076
  363.4 148.3 %copy-start.15 = (f32[256]{0:T(256)S(1)}, f32[256]{0:T(256)}, u32[]{:S(2)}) copy-start(f32[256]{0:T(256)} %get-tuple-element.100) | copy-start | bytes 3076
  363.4 148.3 %copy-start.16 = (f32[256]{0:T(256)S(1)}, f32[256]{0:T(256)}, u32[]{:S(2)}) copy-start(f32[256]{0:T(256)} %get-tuple-element.101) | copy-start | bytes 3076
  363.4 148.3 %copy-start.17 = (f32[256]{0:T(256)S(1)}, f32[256]{0:T(256)}, u32[]{:S(2)}) copy-start(f32[256]{0:T(256)} %get-tuple-element.102) | copy-start | bytes 3076
  379.3 134.3 %copy-start.11 = (f32[256]{0:T(256)S(1)}, f32[256]{0:T(256)}, u32[]{:S(2)}) copy-start(f32[256]{0:T(256)} %copy-done.10) | copy-start | bytes 3076
  379.3 134.3 %copy-start.13 = (f32[256]{0:T(256)S(1)}, f32[256]{0:T(256)}, u32[]{:S(2)}) copy-start(f32[256]{0:T(256)} %copy-done.12) | copy-start | bytes 3076
  379.3 134.4 %copy-start.14 = (f32[256]{0:T(256)S(1)}, f32[256]{0:T(256)}, u32[]{:S(2)}) copy-start(f32[256]{0:T(256)} %get-tuple-element.106) | copy-start | bytes 3076
  507.4 0.7 copy-start.9
Sparse Core Ops, SparseCore 0:
  508.3 255.0 all-reduce.8
where the time goes:
time: 773 us; the launch traced here: 772 us
  blocking collectives  398 us (51%)
  waiting for transfers between devices  249 us (32%)
  local copies, waits for them, and re-layouts  57.5 us (7%)
  other arithmetic  22.1 us (3%)
  starting transfers between devices  21.3 us (3%)
  between operations  15.1 us (2%)
  matrix products  8.32 us (1%)
    unnamed x2, waiting for transfers between devices  249 us
    unnamed x2, blocking collectives  221 us
    all_gather x1, blocking collectives, shards(): lax.all_gather(feature_taps, ('ctx', 'fsdp'), axis=2, tiled=True)  142 us
    all_gather x1, blocking collectives, shards(): filters_all = lax.all_gather(filters, 'ctx', axis=1, tiled=True)  35 us
    ppermute x8, starting transfers between devices, passed_along(): return lax.ppermute(shard, axis, pairs)  21.3 us
  transfers between devices with their start and end apart: 9, of which 1 were waited for; matrix products, arithmetic and copies ran while one was open for 10% of the time, Pallas kernels for 0%

commit v1 on v0

--- a/solution.py
+++ b/solution.py
@@ -1,8 +1,20 @@
+import functools
 import math
 import jax
 import jax.numpy as jnp
 from jax import lax
 from jax.sharding import PartitionSpec as P
+
+
+def assign_sheet(xin, named_axis, where_dim):
+    pages = []
+    for _ in range(lax.axis_size(named_axis)):
+        pages.append(xin)
+    plain = jnp.concatenate(lax.all_to_all(jnp.stack(pages), named_axis, 0, 0), axis=where_dim)
+    return plain
+
+
+grid_settle = functools.partial(assign_sheet, named_axis=("ctx", "fsdp"), where_dim=2)
 
 
 def passed_along(shard, axis, by):
@@ -71,7 +83,7 @@
 def shards(outer_gate, inner_gate, value_stream, grad_output, filters, feature_taps, skip_gain):
     filters_all = lax.all_gather(filters, "ctx", axis=1, tiled=True)
     taps_every, skip_every = (
-        lax.all_gather(feature_taps, ("ctx", "fsdp"), axis=2, tiled=True),
+        grid_settle(feature_taps),
         lax.all_gather(skip_gain, ("ctx", "fsdp"), axis=0, tiled=True),
     )
     channels, block_len = outer_gate.shape

time: 773 us -> 714 us (0.924)
  blocking collectives: 398 us -> 317 us
  starting transfers between devices: 21.3 us -> 42.6 us
    all_gather x1 -> x0, blocking collectives: 142 us -> none  [shards(): lax.all_gather(feature_taps, ('ctx', 'fsdp'), axis=2, tiled=True)]
    all_gather x1, blocking collectives: 35 us -> 90.5 us  [shards(): filters_all = lax.all_gather(filters, 'ctx', axis=1, tiled=True)]
    all_to_all x0 -> x1, starting transfers between devices: none -> 22.1 us  [assign_sheet(): lax.all_to_all(jnp.stack(pages), named_axis, 0, 0)]
    slice x1, local copies, waits for them, and re-layouts: 11.8 us -> 0.09 us  [featurize(): result = tap_gains[0][:, None] * extended[:, 2:]]
  transfers between devices with their start and end apart: 9 -> 10, of which waited for: 1 -> 1; matrix products, arithmetic and copies ran while one was open for 10% -> 10% of each run, Pallas kernels for 0% -> 0%
where the time goes in v1:
time: 714 us; the launch traced here: 712 us
  blocking collectives  317 us (44%)
  waiting for transfers between devices  251 us (35%)
  local copies, waits for them, and re-layouts  56.5 us (8%)
  starting transfers between devices  42.6 us (6%)
  other arithmetic  24.8 us (3%)
  between operations  15.2 us (2%)
    unnamed x2, waiting for transfers between devices  251 us
    unnamed x2, blocking collectives  226 us
    all_gather x1, blocking collectives, shards(): filters_all = lax.all_gather(filters, 'ctx', axis=1, tiled=True)  90.5 us
    all_to_all x1, starting transfers between devices, assign_sheet(): lax.all_to_all(jnp.stack(pages), named_axis, 0, 0)  22.1 us
    ppermute x8, starting transfers between devices, passed_along(): return lax.ppermute(shard, axis, pairs)  20.5 us
  transfers between devices with their start and end apart: 10, of which 1 were waited for; matrix products, arithmetic and copies ran while one was open for 10% of the time, Pallas kernels for 0%

profile of v1, /device:TPU:1, one launch (start us, length us, event | category | flops | bytes accessed | tf_op | source)
XLA Modules:
  0.0 712.0 jit_solution(2965443858461542242)
XLA Ops:
  8.7 4.6 collective-permute-start
  14.9 1.9 collective-permute-start.2
  16.8 2.8 stack.34
  19.6 22.1 %all-to-all-start = ((f32[512,3,3,4]{3,2,1,0:T(4,128)}), f32[512,3,3,4]{3,2,1,0:T(4,128)}, u32[]{:S(2)}, u32[]{:S(2)}) async-start(f32[512,3,3,4]{3,2,1,0:T(4,128)} %stack.34), calls=%async_computation | async-start | bytes 6291456 | tf_op jit(solution)/shard_map/all_to_all | solution.py:13
  42.4 3.5 collective-permute-start.1
  46.0 90.5 %all-gather = bf16[64,2,16]{2,1,0:T(2,128)(2,1)S(1)} all-gather(bf16[1,2,16]{2,1,0:T(2,128)(2,1)S(1)} %bitcast_convert_fusion), channel_id=1, replica_groups=mesh['ctx'=64,'fsdp'=8] {'ctx'}, dimensions={0}, use_global_device_ids=true | all-gather | bytes 4160 | tf_op jit(solution)/shard_map/all_gather | solution.py:84
  137.0 1.9 copy.35
  138.8 1.9 slice.244
  140.7 9.4 %reshape.125 = bf16[16,256,383]{2,1,0:T(8,128)(2,1)S(1)} reshape(bf16[16,98048]{1,0:T(8,128)(2,1)} %slice.244) | data formatting | bytes 6275072 | tf_op jit(solution)/shard_map/reshape | solution.py:62
  152.3 1.7 fusion.35
  154.0 1.7 fusion.36
  155.8 1.7 fusion.37
  157.5 3.5 copy.24
  161.0 3.6 reshape.122
  164.8 3.7 fusion.10
  169.2 1.9 collective-permute-start.3
  173.5 100.7 %all-reduce.6 = (f32[2048]{0:T(1024)}, f32[2048]{0:T(1024)}) all-reduce(f32[2048]{0:T(1024)S(1)} %dynamic-update-slice, f32[2048]{0:T(1024)S(1)} %multiply_dynamic-update-slice_fusion), channel_id=1, replica_groups=mesh['ctx'=64,'fsdp'=8] {'ctx','fsdp'}, use_global_device_ids=true, to_apply=%add.2 | all-reduce | flops 4096 | bytes 32768
  275.0 2.8 collective-permute-start.5
  281.0 2.5 fusion.12
  284.8 1.9 collective-permute-start.4
  289.2 2.5 fusion.41
  291.7 1.9 rev.14
  293.7 2.6 fusion.18
  296.9 1.9 collective-permute-start.6
  299.5 1.9 collective-permute-start.7
  302.4 15.6 %while.12 = (s32[]{:T(128)}, f32[4,4,128]{2,1,0:T(4,128)}, bf16[4,4,16,1,256]{4,2,1,3,0:T(8,128)(2,1)S(1)}, bf16[4,4,16,1,383]{4,2,1,3,0:T(8,128)(2,1)S(1)}, s32[]{:T(128)}, /*index=5*/f32[]{:T(128)}) while((s32[]{:T(128)}, f32[4,4,128]{2,1,0:T(4,128)}, bf16[4,4,16,1,256]{4,2,1,3,0:T(8,128)(2,1)S(1)}, ...), condition=%wide.region_2.3_spmd, body=%wide.region_0.2_spmd.sunk | while | flops 12680706 | bytes 13180045 | solution.py:157
  303.5 1.6 reshape.141
  307.4 1.6 reshape.141
  311.3 1.6 reshape.141
  318.8 125.7 %all-reduce.3 = f32[16,128]{1,0:T(8,128)S(1)} all-reduce(f32[16,128]{1,0:T(8,128)S(1)} %bitcast.110), channel_id=2, replica_groups=mesh['ctx'=64,'fsdp'=8] {'ctx'}, use_global_device_ids=true, to_apply=%region_3.4.clone | all-reduce | flops 2048 | bytes 16384
  447.6 1.7 fusion.27
  453.1 250.6 %all-reduce.9.cloned.1.call-done = f32[3,3,2048]{2,1,0:T(4,128)} async-done(((f32[3,3,2048]{2,1,0:T(4,128)}), f32[3,3,2048]{2,1,0:T(4,128)}) %all-reduce.9.cloned.1.call-update) | async-done | bytes 73744
  (151 shorter events, 38.5 us)
Async XLA Ops:
  8.7 147.0 %collective-permute-start = (bf16[256,2]{1,0:T(8,128)(2,1)}, bf16[256,2]{1,0:T(8,128)(2,1)}, u32[]{:S(2)}, u32[]{:S(2)}) collective-permute-start(bf16[256,2]{1,0:T(8,128)(2,1)} %slice.185), channel_id=1, source_target_pairs={{0,8},{8,16},{16,24},{24,32},{32,40},{40,48},{48,56},{56,64},{64,7... | collective-permute-start | bytes 3080 | tf_op jit(solution)/shard_map/ppermute | solution.py:23
  14.9 137.4 %collective-permute-start.2 = (bf16[256,2]{1,0:T(8,128)(2,1)}, bf16[256,2]{1,0:T(8,128)(2,1)}, u32[]{:S(2)}, u32[]{:S(2)}) collective-permute-start(bf16[256,2]{1,0:T(8,128)(2,1)} %slice.199), channel_id=1, source_target_pairs={{0,8},{8,16},{16,24},{24,32},{32,40},{40,48},{48,56},{56,64},{64,7... | collective-permute-start | bytes 3080 | tf_op jit(solution)/shard_map/ppermute | solution.py:23
  19.6 22.1 %copy-start.7 = (bf16[256,256]{1,0:T(8,128)(2,1)S(1)}, bf16[256,256]{1,0:T(8,128)(2,1)}, u32[]{:S(2)}) copy-start(bf16[256,256]{1,0:T(8,128)(2,1)} %param.10) | copy-start | bytes 393220
  19.6 26.4 %copy-start.28 = (f32[16,2]{0,1:T(2,128)S(1)}, f32[16,2]{0,1:T(2,128)}, u32[]{:S(2)}) copy-start(f32[16,2]{0,1:T(2,128)} %param.13) | copy-start | bytes 388
  19.6 137.9 %all-to-all-start = ((f32[512,3,3,4]{3,2,1,0:T(4,128)}), f32[512,3,3,4]{3,2,1,0:T(4,128)}, u32[]{:S(2)}, u32[]{:S(2)}) async-start(f32[512,3,3,4]{3,2,1,0:T(4,128)} %stack.34), calls=%async_computation | async-start | bytes 6291456 | tf_op jit(solution)/shard_map/all_to_all | solution.py:13
  41.7 662.1 %all-reduce.9.cloned.1.call-start = ((), (), s32[]{:S(2)}) async-start(), calls=%async_computation.1 | async-start | bytes 196608
  42.4 111.6 %collective-permute-start.1 = (bf16[256,2]{1,0:T(8,128)(2,1)}, bf16[256,2]{1,0:T(8,128)(2,1)}, u32[]{:S(2)}, u32[]{:S(2)}) collective-permute-start(bf16[256,2]{1,0:T(8,128)(2,1)} %slice.192), channel_id=1, source_target_pairs={{0,8},{8,16},{16,24},{24,32},{32,40},{40,48},{48,56},{56,64},{64,7... | collective-permute-start | bytes 3080 | tf_op jit(solution)/shard_map/ppermute | solution.py:23
  140.7 11.3 %copy-start.29 = (f32[4]{0:T(128)S(1)}, f32[4]{0:T(128)}, u32[]{:S(2)}) copy-start(f32[4]{0:T(128)} %param.15) | copy-start | bytes 52
  140.7 11.6 %copy-start.6 = (bf16[256,256]{1,0:T(8,128)(2,1)S(1)}, bf16[256,256]{1,0:T(8,128)(2,1)}, u32[]{:S(2)}) copy-start(bf16[256,256]{1,0:T(8,128)(2,1)} %param.11) | copy-start | bytes 393220
  140.7 15.1 %copy-start.3 = (bf16[256,256]{1,0:T(8,128)(2,1)S(1)}, bf16[256,256]{1,0:T(8,128)(2,1)}, u32[]{:S(2)}) copy-start(bf16[256,256]{1,0:T(8,128)(2,1)} %param.9) | copy-start | bytes 393220
  164.7 6.6 copy-start.12
  164.7 6.6 copy-start.14
  164.7 6.6 copy-start.16
  164.7 6.6 copy-start.18
  164.7 6.6 copy-start.20
  164.8 6.6 copy-start.22
  164.8 6.6 copy-start.24
  169.2 109.9 %collective-permute-start.3 = (bf16[256,127]{1,0:T(8,128)(2,1)}, bf16[256,127]{1,0:T(8,128)(2,1)}, u32[]{:S(2)}, u32[]{:S(2)}) collective-permute-start(bf16[256,127]{1,0:T(8,128)(2,1)} %slice.242), channel_id=1, source_target_pairs={{0,8},{8,16},{16,24},{24,32},{32,40},{40,48},{48,56},{56,64},{64,7... | collective-permute-start | bytes 195080 | tf_op jit(solution)/shard_map/ppermute | solution.py:23
  274.2 6.7 copy-start
  274.2 6.7 copy-start.10
  275.0 11.7 %collective-permute-start.5 = (bf16[256,127]{1,0:T(8,128)(2,1)}, bf16[256,127]{1,0:T(8,128)(2,1)S(1)}, u32[]{:S(2)}, u32[]{:S(2)}) collective-permute-start(bf16[256,127]{1,0:T(8,128)(2,1)} %slice.249), channel_id=1, source_target_pairs={{8,0},{16,8},{24,16},{32,24},{40,32},{48,40},{56,48},{64,56},{72,6... | collective-permute-start | bytes 195080 | tf_op jit(solution)/shard_map/ppermute | solution.py:23
  284.8 161.9 %collective-permute-start.4 = (bf16[256,2]{1,0:T(8,128)(2,1)}, bf16[256,2]{1,0:T(8,128)(2,1)}, u32[]{:S(2)}, u32[]{:S(2)}) collective-permute-start(bf16[256,2]{1,0:T(8,128)(2,1)} %slice.245), channel_id=1, source_target_pairs={{8,0},{16,8},{24,16},{32,24},{40,32},{48,40},{56,48},{64,56},{72,6... | collective-permute-start | bytes 3080 | tf_op jit(solution)/shard_map/ppermute | solution.py:23
  296.9 152.3 %collective-permute-start.6 = (bf16[256,2]{1,0:T(8,128)(2,1)}, bf16[256,2]{1,0:T(8,128)(2,1)}, u32[]{:S(2)}, u32[]{:S(2)}) collective-permute-start(bf16[256,2]{1,0:T(8,128)(2,1)} %slice.251), channel_id=1, source_target_pairs={{8,0},{16,8},{24,16},{32,24},{40,32},{48,40},{56,48},{64,56},{72,6... | collective-permute-start | bytes 3080 | tf_op jit(solution)/shard_map/ppermute | solution.py:23
  299.5 151.8 %collective-permute-start.7 = (bf16[256,2]{1,0:T(8,128)(2,1)}, bf16[256,2]{1,0:T(8,128)(2,1)}, u32[]{:S(2)}, u32[]{:S(2)}) collective-permute-start(bf16[256,2]{1,0:T(8,128)(2,1)} %slice.255), channel_id=1, source_target_pairs={{8,0},{16,8},{24,16},{32,24},{40,32},{48,40},{56,48},{64,56},{72,6... | collective-permute-start | bytes 3080 | tf_op jit(solution)/shard_map/ppermute | solution.py:23
  302.4 144.4 %copy-start.5 = (bf16[256,256]{1,0:T(8,128)(2,1)S(1)}, bf16[256,256]{1,0:T(8,128)(2,1)}, u32[]{:S(2)}) copy-start(bf16[256,256]{1,0:T(8,128)(2,1)} %copy-done.4) | copy-start | bytes 393220
  302.4 145.3 %copy-start.25 = (f32[1,1,256]{2,1,0:T(1,128)S(1)}, f32[1,1,256]{2,1,0:T(1,128)}, u32[]{:S(2)}) copy-start(f32[1,1,256]{2,1,0:T(1,128)} %copy-done.24) | copy-start | bytes 3076
  302.4 147.9 %copy-start.19 = (f32[1,1,256]{2,1,0:T(1,128)S(1)}, f32[1,1,256]{2,1,0:T(1,128)}, u32[]{:S(2)}) copy-start(f32[1,1,256]{2,1,0:T(1,128)} %copy-done.18) | copy-start | bytes 3076
  302.4 147.9 %copy-start.21 = (f32[1,1,256]{2,1,0:T(1,128)S(1)}, f32[1,1,256]{2,1,0:T(1,128)}, u32[]{:S(2)}) copy-start(f32[1,1,256]{2,1,0:T(1,128)} %copy-done.20) | copy-start | bytes 3076
  302.4 147.9 %copy-start.23 = (f32[1,1,256]{2,1,0:T(1,128)S(1)}, f32[1,1,256]{2,1,0:T(1,128)}, u32[]{:S(2)}) copy-start(f32[1,1,256]{2,1,0:T(1,128)} %copy-done.22) | copy-start | bytes 3076
  318.0 134.1 %copy-start.13 = (f32[1,1,256]{2,1,0:T(1,128)S(1)}, f32[1,1,256]{2,1,0:T(1,128)}, u32[]{:S(2)}) copy-start(f32[1,1,256]{2,1,0:T(1,128)} %copy-done.12) | copy-start | bytes 3076
  318.0 134.1 %copy-start.15 = (f32[1,1,256]{2,1,0:T(1,128)S(1)}, f32[1,1,256]{2,1,0:T(1,128)}, u32[]{:S(2)}) copy-start(f32[1,1,256]{2,1,0:T(1,128)} %copy-done.14) | copy-start | bytes 3076
  318.0 134.1 %copy-start.17 = (f32[1,1,256]{2,1,0:T(1,128)S(1)}, f32[1,1,256]{2,1,0:T(1,128)}, u32[]{:S(2)}) copy-start(f32[1,1,256]{2,1,0:T(1,128)} %copy-done.16) | copy-start | bytes 3076
  (14 other events, 31.8 us)
Sparse Core Ops, SparseCore 0:
  446.8 256.8 all-reduce.8
